TPU v7x, 256 devices: a whole 4x4x8 slice. The times are simulated.
256 devices in a mesh: sub: 16 (over z, core), fr: 16 (over y, x).
Axes of the slice: x: 4, y: 4, z: 8, core: 2. Of those that a mesh axis runs over, the one named last changes fastest.
Arguments:
- front_leaf: bfloat16 [32768, 2048], P(('sub', 'fr')), as said below
- shares_one: float32 [32768, 384], P(('sub', 'fr')), as said below
- shares_two: float32 [32768, 384], P(('sub', 'fr')), as said below
- map_leaf: int32 [16, 13], P('sub'), may hold values from 0 to 15, as said below
- map_mid: int32 [8, 13], replicated, may hold values from 0 to 15, as said below
Outputs:
- leaf_panel: float32 [32768, 384], P(('sub', 'fr'))
- middle_panel: float32 [32768, 384], P(('sub', 'fr'))
- top_panel: float32 [32768, 384], P(('sub', 'fr'))
- contribution: float32 [32768, 1664], P(('sub', 'fr'))
Inputs may be any that keep to these rules, and one draw needn't show every extreme that they name: `front_leaf`: each block of 2048 rows is a symmetric positive definite front. `shares_one`: in each block of 2048 rows the first 384 rows are symmetric; with the extended contributions every middle front is positive definite. `shares_two`: in each block of 2048 rows the first 384 rows are symmetric; with the extended contributions every top front is positive definite. `map_leaf`: each row lists 13 different blocks; rows 2q and 2q+1 together name every block of their parent. `map_mid`: each row lists 13 different blocks; rows 2r and 2r+1 together name every block of their parent.
All inputs are finite; a program needn't handle non-finite values.
Results may differ from a plain program's by a relative error of at most 0.0003.
Values sent between devices are 32-bit elements; how exact they have to be, the bound alone decides.
No kernel may reach another device: no remote copies, remote signals or barrier semaphores. Data moves between devices by JAX's collectives and lax.ppermute only.
A program may use at most 128 MiB of HBM per device.

v0:
```python
import jax
import jax.numpy as jnp
from jax import lax
from jax.sharding import PartitionSpec as P

BLK = 128
P_SIZE = 384
NFB = 16
NPB = 3
HIGH = lax.Precision.HIGHEST


def partner(array, axis, stride):
    return lax.ppermute(array, axis, [(i, i ^ 1 << stride) for i in range(lax.axis_size(axis))])


def eliminate(front, row_start):
    row_count, front_order = front.shape
    panels = []
    for block_index in range(NPB):
        block_low = block_index * BLK
        gathered = lax.all_gather(front[:, block_low : block_low + BLK], "fr", axis=0, tiled=True)
        row_ids = jnp.arange(front_order)
        lower_block = jnp.linalg.cholesky(gathered[block_low : block_low + BLK])
        solved = lax.linalg.triangular_solve(
            lower_block, gathered, left_side=False, lower=True, transpose_a=True
        )
        below = jnp.where((row_ids >= block_low + BLK)[:, None], solved, 0.0)
        placed = below.at[block_low : block_low + BLK].set(lower_block)
        own_below = lax.dynamic_slice_in_dim(below, row_start, row_count, 0)
        own_panel = lax.dynamic_slice_in_dim(placed, row_start, row_count, 0)
        front = front - jnp.dot(
            own_below, below.T, precision=HIGH, preferred_element_type=jnp.float32
        )
        panels.append(own_panel)
    return (jnp.concatenate(panels, axis=1), front)


def make_table(block_map):
    padded = jnp.concatenate([jnp.full((NPB,), -1, jnp.int32), block_map])
    return (padded[:, None] == jnp.arange(NFB, dtype=jnp.int32)[None, :]).astype(jnp.float32)


def extend(front, block_map, row_start):
    row_count, front_order = front.shape
    block_share = row_count // BLK
    block_table = make_table(block_map)
    padded = jnp.concatenate([jnp.full((NPB,), -1, jnp.int32), block_map])
    parents = row_start // BLK + jnp.arange(block_share)
    matches = padded[None, :] == parents[:, None]
    present = jnp.any(matches, axis=1)
    source_block = jnp.sum(jnp.where(matches, jnp.arange(NFB)[None, :], 0), axis=1)
    source_rows = (source_block[:, None] * BLK + jnp.arange(BLK)[None, :]).reshape(row_count)
    is_live = jnp.repeat(present, BLK)
    shard_rows = lax.all_gather(front, "fr", axis=0, tiled=True)
    inside = is_live & (source_rows >= 0) & (source_rows < shard_rows.shape[0])
    picked_rows = jnp.take(shard_rows, jnp.clip(source_rows, 0, shard_rows.shape[0] - 1), axis=0)
    picked_rows = jnp.where(inside[:, None], picked_rows, 0.0)
    mapped = jnp.einsum(
        "rqc,qe->rec", picked_rows.reshape(row_count, NFB, BLK), block_table, precision=HIGH
    )
    return mapped.reshape(row_count, front_order)


def combine(front, shares, block_map, row_start, level_bit):
    front_order = front.shape[1]
    piece_part = extend(front, block_map, row_start) + jnp.pad(
        shares, ((0, 0), (0, front_order - P_SIZE))
    )
    return piece_part + partner(piece_part, "sub", level_bit)


def local(front_leaf, shares_one, shares_two, map_leaf, map_mid):
    row_count = front_leaf.shape[0]
    row_start = lax.axis_index("fr") * row_count
    sub_index = lax.axis_index("sub")
    leaf_panel, child_front = eliminate(front_leaf.astype(jnp.float32), row_start)
    shares_sum = shares_two + partner(shares_two, "sub", 0)
    middle_front = combine(child_front, shares_one, map_leaf[0], row_start, 0)
    middle_panel, middle_front = eliminate(middle_front, row_start)
    pair_map = lax.dynamic_index_in_dim(map_mid, sub_index // 2, 0, keepdims=False)
    top_front = combine(middle_front, shares_sum, pair_map, row_start, 1)
    top_panel, top_front = eliminate(top_front, row_start)
    row_ids = row_start + jnp.arange(row_count)
    contribution = jnp.where((row_ids >= P_SIZE)[:, None], top_front[:, P_SIZE:], 0.0)
    return (leaf_panel, middle_panel, top_panel, contribution)


def solution(mesh):
    in_specs = (
        P(("sub", "fr"), None),
        P(("sub", "fr"), None),
        P(("sub", "fr"), None),
        P("sub", None),
        P(),
    )
    out_specs = (
        P(("sub", "fr"), None),
        P(("sub", "fr"), None),
        P(("sub", "fr"), None),
        P(("sub", "fr"), None),
    )
    return jax.shard_map(local, mesh=mesh, in_specs=in_specs, out_specs=out_specs, check_vma=False)
```

profile of v0, /device:TPU:2, one launch (start us, length us, event | category | flops | bytes accessed | tf_op | source)
XLA Modules:
  0.0 1077.1 jit_solution(2914424873114445792)
XLA Ops:
  9.3 52.5 %all-gather.12.cloned.1.call-done = f32[2048,128]{0,1:T(8,128)} async-done(((f32[128,128]{0,1:T(8,128)}), f32[2048,128]{0,1:T(8,128)}) %all-gather.12.cloned.1.call-update) | async-done | bytes 1048592 | tf_op jit(solution)/shard_map/all_gather | solution.py:22
  63.6 11.7 %cholesky.149 = f32[128,128]{1,0:T(8,128)S(1)} custom-call(f32[128,128]{1,0:T(8,128)S(1)} %fusion.29), custom_call_target="Cholesky" | custom-call | tf_op jit(solution)/shard_map/jit(cholesky)/cholesky | solution.py:24
  76.6 9.8 custom-call.13
  86.5 2.3 fusion.8
  88.7 1.8 convolution_subtract_fusion.7
  91.5 47.4 %all-gather.14.cloned.1.call-done = f32[2048,128]{0,1:T(8,128)} async-done(((f32[128,128]{0,1:T(8,128)}), f32[2048,128]{0,1:T(8,128)}) %all-gather.14.cloned.1.call-update) | async-done | bytes 1048592 | tf_op jit(solution)/shard_map/all_gather | solution.py:22
  140.7 11.7 %cholesky.160 = f32[128,128]{1,0:T(8,128)S(1)} custom-call(f32[128,128]{1,0:T(8,128)S(1)} %fusion.27), custom_call_target="Cholesky" | custom-call | tf_op jit(solution)/shard_map/jit(cholesky)/cholesky | solution.py:24
  153.8 9.8 custom-call.14
  163.6 2.3 fusion.7
  165.8 1.8 convolution_subtract_fusion.6
  169.8 47.2 %all-gather.16.cloned.1.call-done = f32[2048,128]{0,1:T(8,128)} async-done(((f32[128,128]{0,1:T(8,128)}), f32[2048,128]{0,1:T(8,128)}) %all-gather.16.cloned.1.call-update) | async-done | bytes 1048592 | tf_op jit(solution)/shard_map/all_gather | solution.py:22
  218.8 11.7 %cholesky.171 = f32[128,128]{1,0:T(8,128)S(1)} custom-call(f32[128,128]{1,0:T(8,128)S(1)} %fusion.25), custom_call_target="Cholesky" | custom-call | tf_op jit(solution)/shard_map/jit(cholesky)/cholesky | solution.py:24
  231.9 9.8 custom-call.15
  241.7 2.3 fusion.6
  244.9 4.0 convolution_subtract_fusion.5
  252.2 1.4 compare_reduce_fusion.10
  255.3 118.1 %all-gather.18.cloned.1.call-done = f32[2048,2048]{0,1:T(8,128)} async-done(((f32[128,2048]{0,1:T(8,128)}), f32[2048,2048]{0,1:T(8,128)}) %all-gather.18.cloned.1.call-update) | async-done | bytes 16777232 | tf_op jit(solution)/shard_map/all_gather | solution.py:55
  373.4 17.6 %copy.19 = f32[2048,2048]{1,0:T(8,128)} copy(f32[2048,2048]{0,1:T(8,128)} %all-gather.18.cloned.1.call-done) | data formatting | bytes 33554432 | tf_op jit(solution)/shard_map/all_gather | solution.py:55
  391.0 7.3 gather_fusion
  400.7 1.4 copy.20
  402.1 1.3 bitcast_add_fusion.1
  403.6 2.6 collective-permute-done
  407.0 47.7 %all-gather.20.cloned.1.call-done = f32[2048,128]{0,1:T(8,128)} async-done(((f32[128,128]{0,1:T(8,128)}), f32[2048,128]{0,1:T(8,128)}) %all-gather.20.cloned.1.call-update) | async-done | bytes 1048592 | tf_op jit(solution)/shard_map/all_gather | solution.py:22
  456.5 11.7 %cholesky.182 = f32[128,128]{1,0:T(8,128)S(1)} custom-call(f32[128,128]{1,0:T(8,128)S(1)} %fusion.23), custom_call_target="Cholesky" | custom-call | tf_op jit(solution)/shard_map/jit(cholesky)/cholesky | solution.py:24
  470.2 9.8 custom-call.16
  480.0 2.3 fusion.5
  482.3 1.8 convolution_subtract_fusion.4
  486.0 47.4 %all-gather.22.cloned.1.call-done = f32[2048,128]{0,1:T(8,128)} async-done(((f32[128,128]{0,1:T(8,128)}), f32[2048,128]{0,1:T(8,128)}) %all-gather.22.cloned.1.call-update) | async-done | bytes 1048592 | tf_op jit(solution)/shard_map/all_gather | solution.py:22
  535.2 11.7 %cholesky.193 = f32[128,128]{1,0:T(8,128)S(1)} custom-call(f32[128,128]{1,0:T(8,128)S(1)} %fusion.21), custom_call_target="Cholesky" | custom-call | tf_op jit(solution)/shard_map/jit(cholesky)/cholesky | solution.py:24
  548.9 9.8 custom-call.17
  558.7 2.3 fusion.4
  562.0 3.0 convolution_subtract_fusion.3
  566.1 47.2 %all-gather.24.cloned.1.call-done = f32[2048,128]{0,1:T(8,128)} async-done(((f32[128,128]{0,1:T(8,128)}), f32[2048,128]{0,1:T(8,128)}) %all-gather.24.cloned.1.call-update) | async-done | bytes 1048592 | tf_op jit(solution)/shard_map/all_gather | solution.py:22
  615.2 11.7 %cholesky.204 = f32[128,128]{1,0:T(8,128)S(1)} custom-call(f32[128,128]{1,0:T(8,128)S(1)} %fusion.19), custom_call_target="Cholesky" | custom-call | tf_op jit(solution)/shard_map/jit(cholesky)/cholesky | solution.py:24
  628.8 9.8 custom-call.18
  638.7 2.3 fusion.3
  641.9 2.8 convolution_subtract_fusion.2
  650.6 118.5 %all-gather.26.cloned.1.call-done = f32[2048,2048]{0,1:T(8,128)} async-done(((f32[128,2048]{0,1:T(8,128)}), f32[2048,2048]{0,1:T(8,128)}) %all-gather.26.cloned.1.call-update) | async-done | bytes 16777232 | tf_op jit(solution)/shard_map/all_gather | solution.py:55
  769.2 17.6 %copy.31 = f32[2048,2048]{1,0:T(8,128)} copy(f32[2048,2048]{0,1:T(8,128)} %all-gather.26.cloned.1.call-done) | data formatting | bytes 33554432 | tf_op jit(solution)/shard_map/all_gather | solution.py:55
  786.8 7.3 gather_fusion.1
  796.5 1.4 copy.32
  797.9 1.3 bitcast_add_fusion
  799.3 1.6 collective-permute-start.2
  800.9 22.0 %collective-permute-done.2 = f32[128,2048]{0,1:T(8,128)S(1)} collective-permute-done((f32[128,2048]{0,1:T(8,128)S(1)}, f32[128,2048]{0,1:T(8,128)S(1)}, u32[]{:S(2)}, u32[]{:S(2)}) %collective-permute-start.2) | collective-permute-done | bytes 1048608 | tf_op jit(solution)/shard_map/ppermute | solution.py:14
  823.7 47.7 %all-gather.28.cloned.1.call-done = f32[2048,128]{0,1:T(8,128)} async-done(((f32[128,128]{0,1:T(8,128)}), f32[2048,128]{0,1:T(8,128)}) %all-gather.28.cloned.1.call-update) | async-done | bytes 1048592 | tf_op jit(solution)/shard_map/all_gather | solution.py:22
  871.4 1.5 slice.252
  872.9 1.6 copy.35
  874.4 1.5 fusion.17
  875.9 13.2 %cholesky.215 = f32[128,128]{1,0:T(8,128)} custom-call(f32[128,128]{1,0:T(8,128)} %fusion.17), custom_call_target="Cholesky" | custom-call | tf_op jit(solution)/shard_map/jit(cholesky)/cholesky | solution.py:24
  890.6 2.2 select_bitcast_fusion.2
  892.8 11.3 %custom-call.19 = f32[1,128,128]{1,2,0:T(8,128)} custom-call(f32[1,128,128]{2,1,0:T(8,128)} %get-tuple-element.123), custom_call_target="InvertDiagBlocksLowerTriangular" | custom-call | tf_op jit(solution)/shard_map/triangular_solve/custom-call.0 | solution.py:25
  904.1 2.3 fusion.2
  906.4 1.8 convolution_subtract_fusion.1
  910.9 46.7 %all-gather.30.cloned.1.call-done = f32[2048,128]{0,1:T(8,128)} async-done(((f32[128,128]{0,1:T(8,128)}), f32[2048,128]{0,1:T(8,128)}) %all-gather.30.cloned.1.call-update) | async-done | bytes 1048592 | tf_op jit(solution)/shard_map/all_gather | solution.py:22
  959.4 11.7 %cholesky.226 = f32[128,128]{1,0:T(8,128)S(1)} custom-call(f32[128,128]{1,0:T(8,128)S(1)} %fusion.15), custom_call_target="Cholesky" | custom-call | tf_op jit(solution)/shard_map/jit(cholesky)/cholesky | solution.py:24
  972.5 10.4 custom-call.20
  982.9 2.3 fusion.1
  985.2 3.0 convolution_subtract_fusion
  1003.0 34.7 %all-gather.32.cloned.1.call-done = f32[2048,128]{0,1:T(8,128)} async-done(((f32[128,128]{0,1:T(8,128)}), f32[2048,128]{0,1:T(8,128)}) %all-gather.32.cloned.1.call-update) | async-done | bytes 1048592 | tf_op jit(solution)/shard_map/all_gather | solution.py:22
  1039.4 11.9 %cholesky.237 = f32[128,128]{1,0:T(8,128)S(1)} custom-call(f32[128,128]{1,0:T(8,128)S(1)} %fusion.13), custom_call_target="Cholesky" | custom-call | tf_op jit(solution)/shard_map/jit(cholesky)/cholesky | solution.py:24
  1052.7 9.8 custom-call.21
  1062.5 2.3 fusion
  1064.8 1.8 fusion.31
  1067.6 1.3 fusion.11
  (172 shorter events, 74.6 us)
Async XLA Ops:
  7.2 639.0 %copy-start = (s32[8,13]{1,0:T(8,128)S(1)}, s32[8,13]{1,0:T(8,128)}, u32[]{:S(2)}) copy-start(s32[8,13]{1,0:T(8,128)} %param.32) | copy-start | bytes 1252
  7.2 242.1 %copy-start.13 = (s32[1,13]{1,0:T(1,128)S(1)}, s32[1,13]{1,0:T(1,128)}, u32[]{:S(2)}) copy-start(s32[1,13]{1,0:T(1,128)} %param.31) | copy-start | bytes 160
  7.2 54.6 %all-gather.12.cloned.1.call-start = ((), (), s32[]{:S(2)}) async-start(), calls=%async_computation | async-start | bytes 1114112 | tf_op jit(solution)/shard_map/all_gather | solution.py:22
  9.2 129.7 %all-gather.14.cloned.1.call-start = ((), (), s32[]{:S(2)}) async-start(), calls=%async_computation.1 | async-start | bytes 1114112 | tf_op jit(solution)/shard_map/all_gather | solution.py:22
  91.2 125.8 %all-gather.16.cloned.1.call-start = ((), (), s32[]{:S(2)}) async-start(), calls=%async_computation.2 | async-start | bytes 1114112 | tf_op jit(solution)/shard_map/all_gather | solution.py:22
  167.7 1.0 copy-start.7
  169.3 204.1 %all-gather.18.cloned.1.call-start = ((), (), s32[]{:S(2)}) async-start(), calls=%async_computation.3 | async-start | bytes 17825792 | tf_op jit(solution)/shard_map/all_gather | solution.py:55
  243.9 1.0 copy-start.1
  249.0 205.7 %all-gather.20.cloned.1.call-start = ((), (), s32[]{:S(2)}) async-start(), calls=%async_computation.4 | async-start | bytes 1114112 | tf_op jit(solution)/shard_map/all_gather | solution.py:22
  403.5 2.7 collective-permute-start
  407.0 126.4 %all-gather.22.cloned.1.call-start = ((), (), s32[]{:S(2)}) async-start(), calls=%async_computation.5 | async-start | bytes 1114112 | tf_op jit(solution)/shard_map/all_gather | solution.py:22
  482.2 1.8 copy-start.2
  484.1 1.0 copy-start.8
  485.7 127.6 %all-gather.24.cloned.1.call-start = ((), (), s32[]{:S(2)}) async-start(), calls=%async_computation.6 | async-start | bytes 1114112 | tf_op jit(solution)/shard_map/all_gather | solution.py:22
  561.0 1.0 copy-start.3
  565.7 203.5 %all-gather.26.cloned.1.call-start = ((), (), s32[]{:S(2)}) async-start(), calls=%async_computation.7 | async-start | bytes 17825792 | tf_op jit(solution)/shard_map/all_gather | solution.py:55
  640.9 1.0 copy-start.4
  644.8 226.6 %all-gather.28.cloned.1.call-start = ((), (), s32[]{:S(2)}) async-start(), calls=%async_computation.8 | async-start | bytes 1114112 | tf_op jit(solution)/shard_map/all_gather | solution.py:22
  645.9 4.7 collective-permute-start.1
  799.2 195.6 %copy-start.10 = (f32[128,128]{1,0:T(8,128)S(1)}, f32[128,128]{1,0:T(8,128)}, u32[]{:S(2)}) copy-start(f32[128,128]{1,0:T(8,128)} %get-tuple-element.130) | copy-start | bytes 196612
  799.3 197.1 %copy-start.11 = (f32[128,128]{1,0:T(8,128)S(1)}, f32[128,128]{1,0:T(8,128)}, u32[]{:S(2)}) copy-start(f32[128,128]{1,0:T(8,128)} %get-tuple-element.128) | copy-start | bytes 196612
  799.3 198.7 %copy-start.12 = (f32[128,128]{1,0:T(8,128)S(1)}, f32[128,128]{1,0:T(8,128)}, u32[]{:S(2)}) copy-start(f32[128,128]{1,0:T(8,128)} %get-tuple-element.126) | copy-start | bytes 196612
  799.3 23.6 %collective-permute-start.2 = (f32[128,2048]{0,1:T(8,128)S(1)}, f32[128,2048]{0,1:T(8,128)S(1)}, u32[]{:S(2)}, u32[]{:S(2)}) collective-permute-start(f32[128,2048]{0,1:T(8,128)S(1)} %bitcast_add_fusion), channel_id=1, source_target_pairs={{0,32},{16,48},{32,0},{48,16},{64,96},{80,112},{96,64},{112,80},{1... | collective-permute-start | bytes 3145736 | tf_op jit(solution)/shard_map/ppermute | solution.py:14
  823.7 133.9 %all-gather.30.cloned.1.call-start = ((), (), s32[]{:S(2)}) async-start(), calls=%async_computation.9 | async-start | bytes 1114112 | tf_op jit(solution)/shard_map/all_gather | solution.py:22
  906.4 1.8 copy-start.5
  908.2 1.0 copy-start.6
  909.9 127.7 %all-gather.32.cloned.1.call-start = ((), (), s32[]{:S(2)}) async-start(), calls=%async_computation.10 | async-start | bytes 1114112 | tf_op jit(solution)/shard_map/all_gather | solution.py:22
  988.2 1.0 copy-start.9
Sparse Core Ops, SparseCore 0:
  11.0 50.7 all-gather.11
  91.3 47.5 all-gather.13
  169.4 47.5 all-gather.15
  249.1 124.2 all-gather.17
  407.1 47.5 all-gather.19
  485.9 47.5 all-gather.21
  565.8 47.5 all-gather.23
  644.9 124.2 all-gather.25
  823.8 47.5 all-gather.27
  910.0 47.5 all-gather.29
  990.1 47.5 all-gather.31
where the time goes:
time: 1090 us; the launch traced here: 1080 us
  waiting for transfers between devices  680 us (62%)
  other arithmetic  237 us (22%)
  local copies, waits for them, and re-layouts  94.7 us (9%)
  matrix products  44.9 us (4%)
  between operations  16.4 us (2%)
    all_gather x9, waiting for transfers between devices, eliminate(): lax.all_gather(front[:, block_low:block_low + BLK], 'fr', axis=0, tiled=T...  419 us
    all_gather x2, waiting for transfers between devices, extend(): shard_rows = lax.all_gather(front, 'fr', axis=0, tiled=True)  237 us
    another operation x27, other arithmetic, eliminate(): lower_block = jnp.linalg.cholesky(gathered[block_low:block_low + BLK])  114 us
    another operation x18, other arithmetic, eliminate(): lax.linalg.triangular_solve(lower_block, gathered, left_side=False, lower...  99.7 us
    all_gather x2, local copies, waits for them, and re-layouts, extend(): shard_rows = lax.all_gather(front, 'fr', axis=0, tiled=True)  35.2 us
    ppermute x3, waiting for transfers between devices, partner(): lax.ppermute(array, axis, [(i, i ^ 1 << stride) for i in range(lax.axis_s...  24.6 us
    dot_general x9, matrix products, eliminate(): jnp.dot(own_below, below.T, precision=HIGH, preferred_element_type=jnp.fl...  22 us
  transfers between devices with their start and end apart: 14, of which 13 were waited for; matrix products, arithmetic and copies ran while one was open for 2% of the time, Pallas kernels for 0%

commit v1 on v0

--- a/solution.py
+++ b/solution.py
@@ -19,7 +19,12 @@
     panels = []
     for block_index in range(NPB):
         block_low = block_index * BLK
-        gathered = lax.all_gather(front[:, block_low : block_low + BLK], "fr", axis=0, tiled=True)
+        gathered = jnp.concatenate(
+            lax.all_to_all(
+                jnp.stack([front[:, block_low : block_low + BLK]] * lax.axis_size("fr")), "fr", 0, 0
+            ),
+            axis=0,
+        )
         row_ids = jnp.arange(front_order)
         lower_block = jnp.linalg.cholesky(gathered[block_low : block_low + BLK])
         solved = lax.linalg.triangular_solve(

time: 1090 us -> 761 us (0.70)
  waiting for transfers between devices: 680 us -> 308 us
  blocking collectives: 0 us -> 81.3 us
  local copies, waits for them, and re-layouts: 94.7 us -> 53.1 us
  starting transfers between devices: 4.07 us -> 31 us
  matrix products: 44.9 us -> 33 us
    all_gather x9 -> x0, waiting for transfers between devices: 419 us -> none  [eliminate(): lax.all_gather(front[:, block_low:block_low + BLK], 'fr', axis=0, tiled=T...]
    all_to_all x0 -> x4, blocking collectives: none -> 81.3 us  [eliminate(): lax.all_to_all(jnp.stack([front[:, block_low:block_low + BLK]] * lax.axis...]
    all_to_all x0 -> x5, waiting for transfers between devices: none -> 58.8 us  [eliminate(): lax.all_to_all(jnp.stack([front[:, block_low:block_low + BLK]] * lax.axis...]
    all_gather x2 -> x0, local copies, waits for them, and re-layouts: 35.2 us -> none  [extend(): shard_rows = lax.all_gather(front, 'fr', axis=0, tiled=True)]
    all_to_all x0 -> x5, starting transfers between devices: none -> 28.5 us  [eliminate(): lax.all_to_all(jnp.stack([front[:, block_low:block_low + BLK]] * lax.axis...]
    all_gather x2, waiting for transfers between devices: 237 us -> 223 us  [extend(): shard_rows = lax.all_gather(front, 'fr', axis=0, tiled=True)]
  transfers between devices with their start and end apart: 14 -> 10, of which waited for: 13 -> 9; matrix products, arithmetic and copies ran while one was open for 2% -> 3% of each run, Pallas kernels for 0% -> 0%
where the time goes in v1:
time: 761 us; the launch traced here: 751 us
  waiting for transfers between devices  308 us (40%)
  other arithmetic  229 us (30%)
  blocking collectives  81.3 us (11%)
  local copies, waits for them, and re-layouts  53.1 us (7%)
  matrix products  33 us (4%)
  starting transfers between devices  31 us (4%)
  between operations  16.8 us (2%)
    all_gather x2, waiting for transfers between devices, extend(): shard_rows = lax.all_gather(front, 'fr', axis=0, tiled=True)  223 us
    another operation x27, other arithmetic, eliminate(): lower_block = jnp.linalg.cholesky(gathered[block_low:block_low + BLK])  114 us
    another operation x18, other arithmetic, eliminate(): lax.linalg.triangular_solve(lower_block, gathered, left_side=False, lower...  101 us
    all_to_all x4, blocking collectives, eliminate(): lax.all_to_all(jnp.stack([front[:, block_low:block_low + BLK]] * lax.axis...  81.3 us
    all_to_all x5, waiting for transfers between devices, eliminate(): lax.all_to_all(jnp.stack([front[:, block_low:block_low + BLK]] * lax.axis...  58.8 us
    all_to_all x5, starting transfers between devices, eliminate(): lax.all_to_all(jnp.stack([front[:, block_low:block_low + BLK]] * lax.axis...  28.5 us
    ppermute x3, waiting for transfers between devices, partner(): lax.ppermute(array, axis, [(i, i ^ 1 << stride) for i in range(lax.axis_s...  25.8 us
    dot_general x9, matrix products, eliminate(): jnp.dot(own_below, below.T, precision=HIGH, preferred_element_type=jnp.fl...  16.3 us
  transfers between devices with their start and end apart: 10, of which 9 were waited for; matrix products, arithmetic and copies ran while one was open for 3% of the time, Pallas kernels for 0%

profile of v1, /device:TPU:2, one launch (start us, length us, event | category | flops | bytes accessed | tf_op | source)
XLA Modules:
  0.0 751.5 jit_solution(5482227822007001319)
XLA Ops:
  9.1 7.5 all-to-all-start
  16.6 15.8 %all-to-all-done = f32[16,128,128]{1,2,0:T(8,128)S(1)} async-done(((f32[16,128,128]{1,2,0:T(8,128)}), f32[16,128,128]{1,2,0:T(8,128)S(1)}, u32[]{:S(2)}, u32[]{:S(2)}) %all-to-all-start) | async-done | bytes 1048608 | tf_op jit(solution)/shard_map/all_to_all | solution.py:23
  32.5 11.7 %cholesky.149 = f32[128,128]{1,0:T(8,128)S(1)} custom-call(f32[128,128]{1,0:T(8,128)S(1)} %fusion.20), custom_call_target="Cholesky" | custom-call | tf_op jit(solution)/shard_map/jit(cholesky)/cholesky | solution.py:29
  45.6 9.8 %custom-call.13 = f32[1,128,128]{1,2,0:T(8,128)S(1)} custom-call(f32[1,128,128]{2,1,0:T(8,128)S(1)} %get-tuple-element.139), custom_call_target="InvertDiagBlocksLowerTriangular" | custom-call | tf_op jit(solution)/shard_map/triangular_solve/custom-call.0 | solution.py:30
  56.8 2.1 convolution_subtract_fusion.7
  60.1 1.1 stack.19
  61.2 5.7 all-to-all-start.1
  66.9 15.0 %all-to-all-done.1 = f32[16,128,128]{1,2,0:T(8,128)S(1)} async-done(((f32[16,128,128]{1,2,0:T(8,128)}), f32[16,128,128]{1,2,0:T(8,128)S(1)}, u32[]{:S(2)}, u32[]{:S(2)}) %all-to-all-start.1) | async-done | bytes 1048608 | tf_op jit(solution)/shard_map/all_to_all | solution.py:23
  82.1 11.7 %cholesky.160 = f32[128,128]{1,0:T(8,128)S(1)} custom-call(f32[128,128]{1,0:T(8,128)S(1)} %fusion.19), custom_call_target="Cholesky" | custom-call | tf_op jit(solution)/shard_map/jit(cholesky)/cholesky | solution.py:29
  95.1 9.8 %custom-call.14 = f32[1,128,128]{1,2,0:T(8,128)S(1)} custom-call(f32[1,128,128]{2,1,0:T(8,128)S(1)} %get-tuple-element.137), custom_call_target="InvertDiagBlocksLowerTriangular" | custom-call | tf_op jit(solution)/shard_map/triangular_solve/custom-call.0 | solution.py:30
  107.4 2.3 convolution_subtract_fusion.6
  110.9 4.8 all-to-all-start.2
  116.2 14.7 %all-to-all-done.2 = f32[16,128,128]{1,2,0:T(8,128)S(1)} async-done(((f32[16,128,128]{1,2,0:T(8,128)}), f32[16,128,128]{1,2,0:T(8,128)S(1)}, u32[]{:S(2)}, u32[]{:S(2)}) %all-to-all-start.2) | async-done | bytes 1048608 | tf_op jit(solution)/shard_map/all_to_all | solution.py:23
  131.0 11.7 %cholesky.171 = f32[128,128]{1,0:T(8,128)S(1)} custom-call(f32[128,128]{1,0:T(8,128)S(1)} %fusion.18), custom_call_target="Cholesky" | custom-call | tf_op jit(solution)/shard_map/jit(cholesky)/cholesky | solution.py:29
  143.4 1.3 select_bitcast_fusion.6
  144.7 11.3 %custom-call.15 = f32[1,128,128]{1,2,0:T(8,128)} custom-call(f32[1,128,128]{2,1,0:T(8,128)} %get-tuple-element.135), custom_call_target="InvertDiagBlocksLowerTriangular" | custom-call | tf_op jit(solution)/shard_map/triangular_solve/custom-call.0 | solution.py:30
  156.0 1.3 copy.49
  157.3 2.3 fusion.6
  160.6 2.1 convolution_subtract_fusion.5
  162.8 1.4 fusion.63
  164.8 1.4 compare_reduce_fusion.10
  166.9 112.2 %all-gather.3.cloned.1.call-done = f32[2048,2048]{1,0:T(8,128)} async-done(((f32[128,2048]{1,0:T(8,128)}), f32[2048,2048]{1,0:T(8,128)}) %all-gather.3.cloned.1.call-update) | async-done | bytes 16777232 | tf_op jit(solution)/shard_map/all_gather | solution.py:60
  279.0 7.2 gather_fusion
  287.8 2.6 collective-permute-done
  290.8 21.6 %all_to_all.45 = f32[16,128,128]{1,2,0:T(8,128)S(1)} all-to-all(f32[16,128,128]{1,2,0:T(8,128)S(1)} %stack.21), channel_id=1, replica_groups=mesh['sub'=16,'fr'=16] {'fr'}, dimensions={0} | all-to-all | bytes 2097152 | tf_op jit(solution)/shard_map/all_to_all | solution.py:23
  312.5 11.7 %cholesky.182 = f32[128,128]{1,0:T(8,128)S(1)} custom-call(f32[128,128]{1,0:T(8,128)S(1)} %fusion.17), custom_call_target="Cholesky" | custom-call | tf_op jit(solution)/shard_map/jit(cholesky)/cholesky | solution.py:29
  325.5 9.8 %custom-call.16 = f32[1,128,128]{1,2,0:T(8,128)S(1)} custom-call(f32[1,128,128]{2,1,0:T(8,128)S(1)} %get-tuple-element.133), custom_call_target="InvertDiagBlocksLowerTriangular" | custom-call | tf_op jit(solution)/shard_map/triangular_solve/custom-call.0 | solution.py:30
  335.4 1.4 copy.53
  336.7 2.3 fusion.5
  340.3 19.8 %all_to_all.46 = f32[16,128,128]{1,2,0:T(8,128)S(1)} all-to-all(f32[16,128,128]{1,2,0:T(8,128)S(1)} %stack.22), channel_id=1, replica_groups=mesh['sub'=16,'fr'=16] {'fr'}, dimensions={0} | all-to-all | bytes 2097152 | tf_op jit(solution)/shard_map/all_to_all | solution.py:23
  360.3 11.7 %cholesky.193 = f32[128,128]{1,0:T(8,128)S(1)} custom-call(f32[128,128]{1,0:T(8,128)S(1)} %fusion.16), custom_call_target="Cholesky" | custom-call | tf_op jit(solution)/shard_map/jit(cholesky)/cholesky | solution.py:29
  372.7 1.3 select_bitcast_fusion.4
  373.9 10.6 %custom-call.17 = f32[1,128,128]{1,2,0:T(8,128)S(1)} custom-call(f32[1,128,128]{2,1,0:T(8,128)} %get-tuple-element.131), custom_call_target="InvertDiagBlocksLowerTriangular" | custom-call | tf_op jit(solution)/shard_map/triangular_solve/custom-call.0 | solution.py:30
  384.6 1.4 copy.57
  386.0 2.3 fusion.4
  391.5 19.5 %all_to_all.47 = f32[16,128,128]{1,2,0:T(8,128)S(1)} all-to-all(f32[16,128,128]{1,2,0:T(8,128)S(1)} %stack.23), channel_id=1, replica_groups=mesh['sub'=16,'fr'=16] {'fr'}, dimensions={0} | all-to-all | bytes 2097152 | tf_op jit(solution)/shard_map/all_to_all | solution.py:23
  411.2 11.7 %cholesky.204 = f32[128,128]{1,0:T(8,128)S(1)} custom-call(f32[128,128]{1,0:T(8,128)S(1)} %fusion.15), custom_call_target="Cholesky" | custom-call | tf_op jit(solution)/shard_map/jit(cholesky)/cholesky | solution.py:29
  424.2 10.4 %custom-call.18 = f32[1,128,128]{1,2,0:T(8,128)} custom-call(f32[1,128,128]{2,1,0:T(8,128)S(1)} %get-tuple-element.129), custom_call_target="InvertDiagBlocksLowerTriangular" | custom-call | tf_op jit(solution)/shard_map/triangular_solve/custom-call.0 | solution.py:30
  435.0 1.9 fusion.3
  438.0 3.3 convolution_subtract_fusion.2
  445.1 110.9 %all-gather.5.cloned.1.call-done = f32[2048,2048]{1,0:T(8,128)} async-done(((f32[128,2048]{1,0:T(8,128)}), f32[2048,2048]{1,0:T(8,128)}) %all-gather.5.cloned.1.call-update) | async-done | bytes 16777232 | tf_op jit(solution)/shard_map/all_gather | solution.py:60
  556.0 7.2 gather_fusion.1
  564.6 1.8 collective-permute-start.2
  566.4 23.2 %collective-permute-done.2 = f32[128,2048]{1,0:T(8,128)S(1)} collective-permute-done((f32[128,2048]{1,0:T(8,128)S(1)}, f32[128,2048]{1,0:T(8,128)S(1)}, u32[]{:S(2)}, u32[]{:S(2)}) %collective-permute-start.2) | collective-permute-done | bytes 1048608 | tf_op jit(solution)/shard_map/ppermute | solution.py:14
  590.0 20.4 %all_to_all.48 = f32[16,128,128]{1,2,0:T(8,128)S(1)} all-to-all(f32[16,128,128]{1,2,0:T(8,128)S(1)} %stack.24), channel_id=1, replica_groups=mesh['sub'=16,'fr'=16] {'fr'}, dimensions={0} | all-to-all | bytes 2097152 | tf_op jit(solution)/shard_map/all_to_all | solution.py:23
  611.0 1.6 copy.64
  612.5 1.5 fusion.14
  614.0 13.2 %cholesky.215 = f32[128,128]{1,0:T(8,128)} custom-call(f32[128,128]{1,0:T(8,128)} %fusion.14), custom_call_target="Cholesky" | custom-call | tf_op jit(solution)/shard_map/jit(cholesky)/cholesky | solution.py:29
  628.7 2.2 select_bitcast_fusion.2
  630.9 11.3 %custom-call.19 = f32[1,128,128]{1,2,0:T(8,128)} custom-call(f32[1,128,128]{2,1,0:T(8,128)} %get-tuple-element.127), custom_call_target="InvertDiagBlocksLowerTriangular" | custom-call | tf_op jit(solution)/shard_map/triangular_solve/custom-call.0 | solution.py:30
  642.2 1.3 copy.65
  643.5 2.3 fusion.2
  649.1 5.2 all-to-all-start.7
  661.4 1.5 constant_dynamic-slice_fusion.6
  662.9 5.7 all-to-all-done.7
  668.7 11.7 %cholesky.226 = f32[128,128]{1,0:T(8,128)S(1)} custom-call(f32[128,128]{1,0:T(8,128)S(1)} %fusion.13), custom_call_target="Cholesky" | custom-call | tf_op jit(solution)/shard_map/jit(cholesky)/cholesky | solution.py:29
  681.8 9.8 %custom-call.20 = f32[1,128,128]{1,2,0:T(8,128)S(1)} custom-call(f32[1,128,128]{2,1,0:T(8,128)S(1)} %get-tuple-element.125), custom_call_target="InvertDiagBlocksLowerTriangular" | custom-call | tf_op jit(solution)/shard_map/triangular_solve/custom-call.0 | solution.py:30
  693.0 2.3 convolution_subtract_fusion
  695.5 1.2 stack.26
  696.7 5.2 all-to-all-start.8
  707.8 7.6 %all-to-all-done.8 = f32[16,128,128]{1,2,0:T(8,128)S(1)} async-done(((f32[16,128,128]{1,2,0:T(8,128)}), f32[16,128,128]{1,2,0:T(8,128)S(1)}, u32[]{:S(2)}, u32[]{:S(2)}) %all-to-all-start.8) | async-done | bytes 1048608 | tf_op jit(solution)/shard_map/all_to_all | solution.py:23
  715.6 11.7 %cholesky.237 = f32[128,128]{1,0:T(8,128)S(1)} custom-call(f32[128,128]{1,0:T(8,128)S(1)} %fusion.12), custom_call_target="Cholesky" | custom-call | tf_op jit(solution)/shard_map/jit(cholesky)/cholesky | solution.py:29
  728.6 9.8 %custom-call.21 = f32[1,128,128]{1,2,0:T(8,128)S(1)} custom-call(f32[1,128,128]{2,1,0:T(8,128)S(1)} %get-tuple-element.123), custom_call_target="InvertDiagBlocksLowerTriangular" | custom-call | tf_op jit(solution)/shard_map/triangular_solve/custom-call.0 | solution.py:30
  741.9 2.3 fusion.11
  (171 shorter events, 56.1 us)
Async XLA Ops:
  7.2 434.2 %copy-start = (s32[8,13]{1,0:T(8,128)S(1)}, s32[8,13]{1,0:T(8,128)}, u32[]{:S(2)}) copy-start(s32[8,13]{1,0:T(8,128)} %param.32) | copy-start | bytes 1252
  9.1 23.3 %all-to-all-start = ((f32[16,128,128]{1,2,0:T(8,128)}), f32[16,128,128]{1,2,0:T(8,128)S(1)}, u32[]{:S(2)}, u32[]{:S(2)}) async-start(f32[16,128,128]{1,2,0:T(8,128)} %stack.18), calls=%async_computation | async-start | bytes 2097152 | tf_op jit(solution)/shard_map/all_to_all | solution.py:23
  59.0 1.0 copy-start.7
  61.2 20.7 %all-to-all-start.1 = ((f32[16,128,128]{1,2,0:T(8,128)}), f32[16,128,128]{1,2,0:T(8,128)S(1)}, u32[]{:S(2)}, u32[]{:S(2)}) async-start(f32[16,128,128]{1,2,0:T(8,128)} %stack.19), calls=%async_computation.1 | async-start | bytes 2097152 | tf_op jit(solution)/shard_map/all_to_all | solution.py:23
  106.4 1.0 copy-start.1
  110.9 20.0 %all-to-all-start.2 = ((f32[16,128,128]{1,2,0:T(8,128)}), f32[16,128,128]{1,2,0:T(8,128)S(1)}, u32[]{:S(2)}, u32[]{:S(2)}) async-start(f32[16,128,128]{1,2,0:T(8,128)} %stack.20), calls=%async_computation.2 | async-start | bytes 2097152 | tf_op jit(solution)/shard_map/all_to_all | solution.py:23
  115.7 163.3 %all-gather.3.cloned.1.call-start = ((), (), s32[]{:S(2)}) async-start(), calls=%async_computation.9 | async-start | bytes 17825792 | tf_op jit(solution)/shard_map/all_gather | solution.py:60
  144.7 142.6 %copy-start.10 = (f32[128,384]{1,0:T(8,128)S(1)}, f32[128,384]{1,0:T(8,128)}, u32[]{:S(2)}) copy-start(f32[128,384]{1,0:T(8,128)} %param.29) | copy-start | bytes 589828
  159.6 1.0 copy-start.2
  162.7 393.3 %all-gather.5.cloned.1.call-start = ((), (), s32[]{:S(2)}) async-start(), calls=%async_computation.10 | async-start | bytes 17825792 | tf_op jit(solution)/shard_map/all_gather | solution.py:60
  287.7 2.7 collective-permute-start
  339.0 1.1 copy-start.4
  388.3 1.0 copy-start.3
  390.3 1.0 copy-start.8
  436.9 1.0 copy-start.5
  441.3 2.9 collective-permute-start.1
  564.6 25.0 %collective-permute-start.2 = (f32[128,2048]{1,0:T(8,128)S(1)}, f32[128,2048]{1,0:T(8,128)S(1)}, u32[]{:S(2)}, u32[]{:S(2)}) collective-permute-start(f32[128,2048]{1,0:T(8,128)S(1)} %bitcast_add_fusion), channel_id=1, source_target_pairs={{0,32},{16,48},{32,0},{48,16},{64,96},{80,112},{96,64},{112,80},{1... | collective-permute-start | bytes 3145736 | tf_op jit(solution)/shard_map/ppermute | solution.py:14
  646.9 1.0 copy-start.6
  649.1 19.5 %all-to-all-start.7 = ((f32[16,128,128]{1,2,0:T(8,128)}), f32[16,128,128]{1,2,0:T(8,128)S(1)}, u32[]{:S(2)}, u32[]{:S(2)}) async-start(f32[16,128,128]{1,2,0:T(8,128)} %stack.25), calls=%async_computation.7 | async-start | bytes 2097152 | tf_op jit(solution)/shard_map/all_to_all | solution.py:23
  695.3 1.4 copy-start.9
  696.7 18.8 %all-to-all-start.8 = ((f32[16,128,128]{1,2,0:T(8,128)}), f32[16,128,128]{1,2,0:T(8,128)S(1)}, u32[]{:S(2)}, u32[]{:S(2)}) async-start(f32[16,128,128]{1,2,0:T(8,128)} %stack.26), calls=%async_computation.8 | async-start | bytes 2097152 | tf_op jit(solution)/shard_map/all_to_all | solution.py:23
Sparse Core Ops, SparseCore 0:
  162.9 116.1 all-gather.2
  441.4 114.5 all-gather.4
